TPU v7x, 512 devices: a whole 4x8x8 slice. The times are simulated.
512 devices in a mesh: grp: 16 (over z, core), shard: 32 (over x, y).
Axes of the slice: x: 4, y: 8, z: 8, core: 2. Of those that a mesh axis runs over, the one named last changes fastest.
Arguments:
- src_rows: bfloat16 [128, 128, 5376], P('grp', 'shard'), may hold values from -6 to 6
- src_act: bfloat16 [128, 128], P('grp', 'shard'), may hold values from 0.29882812 to 3
- encoder: bfloat16 [16, 32, 3, 5376, 128], P('grp', 'shard'), may hold values from -0.078125 to 0.078125
- dest_list: int32 [16, 6], replicated, may hold values from -1 to 127, as said below
- pair_list: int32 [16, 32, 18, 2], P('grp', 'shard'), may hold values from 0 to 5, as said below
- pair_count: int32 [16, 32], P('grp', 'shard'), may hold values from 1 to 18, as said below
Outputs:
- edges: bfloat16 [16, 32, 18, 128, 128], P('grp', 'shard')
Inputs may be any that keep to these rules, and one draw needn't show every extreme that they name: `dest_list`: row g holds between 3 and 6 source blocks followed by -1; the blocks of one row come from distinct source groups (block // 8); some row is full. `pair_list`: entries are (slot, encoder block) with slot < 6 and block < 3; the first pair_count entries of a device are distinct pairs whose slot holds a block of its group. `pair_count`: at most 3 times the number of blocks of the device's group; some device has 18.
All inputs are finite; a program needn't handle non-finite values.
Results may differ from a plain program's by a relative error of at most 0.001.
Values may be sent and summed in bfloat16 or wider, within the bound.
No kernel may reach another device: no remote copies, remote signals or barrier semaphores. Data moves between devices by JAX's collectives and lax.ppermute only.
A program may use at most 64 MiB of HBM per device.

v0:
```python
import jax
import jax.numpy as jnp
from jax import lax
from jax.sharding import PartitionSpec as P


def local(src_rows, src_act, encoder, dest_list, pair_list, pair_count):
    my_group = lax.axis_index("grp")
    my_list = lax.dynamic_index_in_dim(dest_list, my_group, 0, keepdims=False)
    is_valid = my_list >= 0
    picked = jnp.maximum(my_list, 0)
    all_rows, all_scale = (
        lax.all_gather(src_rows, "grp", axis=0, tiled=True),
        lax.all_gather(src_act, "grp", axis=0, tiled=True),
    )
    slot_rows = jnp.take(all_rows, picked, axis=0)
    slot_scale = jnp.take(all_scale, picked, axis=0)
    slot_rows = jnp.where(is_valid[:, None, None], slot_rows, jnp.zeros((), slot_rows.dtype))
    slot_scale = jnp.where(is_valid[:, None], slot_scale, jnp.zeros((), slot_scale.dtype))
    full_rows, full_scale = (
        lax.all_gather(slot_rows, "shard", axis=1, tiled=True),
        lax.all_gather(slot_scale, "shard", axis=1, tiled=True),
    )
    weights = encoder[0, 0]
    dev_pairs = pair_list[0, 0]
    slot_ids = dev_pairs[:, 0]
    block_ids = dev_pairs[:, 1]
    amount = pair_count[0, 0]
    slots_total = full_rows.shape[0]
    tile_rows = full_rows.shape[1]
    width = full_rows.shape[2]
    enc_count = weights.shape[0]
    tile_cols = weights.shape[2]
    pair_total = dev_pairs.shape[0]
    stacked = full_rows.reshape(slots_total * tile_rows, width)
    products = jnp.einsum("rd,edc->rec", stacked, weights, preferred_element_type=jnp.float32)
    products = products.reshape(slots_total, tile_rows, enc_count, tile_cols)
    chosen = products[slot_ids, :, block_ids, :]
    scales = jnp.take(full_scale, slot_ids, axis=0).astype(jnp.float32)
    is_live = jnp.arange(pair_total) < amount
    result = jnp.where(
        is_live[:, None, None], scales[:, :, None] * chosen, jnp.zeros((), jnp.float32)
    ).astype(jnp.bfloat16)
    return result[None, None]


def solution(mesh):
    return jax.shard_map(
        local,
        mesh=mesh,
        in_specs=(
            P("grp", "shard", None),
            P("grp", "shard"),
            P("grp", "shard", None, None, None),
            P(),
            P("grp", "shard", None, None),
            P("grp", "shard"),
        ),
        out_specs=P("grp", "shard", None, None, None),
        check_vma=False,
    )
```

profile of v0, /device:TPU:1, one launch (start us, length us, event | category | flops | bytes accessed | tf_op | source)
XLA Modules:
  0.0 197.3 jit_solution(8817233090064426488)
XLA Ops:
  6.5 0.0 copy-start
  6.5 0.0 all-gather.5.cloned.1.call-start
  6.5 0.7 all-gather.5.cloned.1.call-update
  7.3 0.0 copy-start.1
  7.3 0.0 all-gather.7.cloned.1.call-start
  7.3 0.9 maximum_reduce_fusion
  8.2 0.9 compare_reduce_fusion.1
  9.1 53.5 %all-gather.5.cloned.1.call-done = bf16[128,4,5376]{2,1,0:T(4,128)(2,1)} async-done(((bf16[8,4,5376]{2,1,0:T(4,128)(2,1)}), bf16[128,4,5376]{2,1,0:T(4,128)(2,1)}) %all-gather.5.cloned.1.call-update) | async-done | bytes 5505040 | tf_op jit(solution)/shard_map/all_gather | solution.py:13
  62.6 3.3 %gather_fusion.2 = bf16[6,4,5376]{2,1,0:T(4,128)(2,1)S(1)} fusion(bf16[128,4,5376]{2,1,0:T(4,128)(2,1)} %all-gather.5.cloned.1.call-done, s32[1024]{0:T(1024)S(1)} %pad_clamp_fusion.1), kind=kCustom, calls=%fused_computation.2 | custom fusion | bytes 516120 | tf_op jit(solution)/shard_map/jit(_take)/gather | solution.py:16
  65.9 0.2 select_select_fusion
  66.2 0.8 copy.16
  66.9 0.0 all-gather.7.cloned.1.call-update
  67.0 0.0 copy-done
  67.0 16.3 %all-gather = bf16[16,8,4]{1,2,0:T(4,128)(2,1)S(1)} all-gather(bf16[1,8,4]{1,2,0:T(4,128)(2,1)S(1)} %bitcast.32), channel_id=1, replica_groups=mesh['grp'=16,'shard'=32] {'grp'}, dimensions={0}, use_global_device_ids=true | all-gather | bytes 1088 | tf_op jit(solution)/shard_map/all_gather | solution.py:14
  83.3 0.2 copy.13
  83.5 0.6 gather_fusion
  84.0 0.1 select_bitcast_fusion
  84.1 0.1 copy.14
  84.2 33.3 %all-gather.1 = bf16[32,4,6]{2,1,0:T(4,128)(2,1)S(1)} all-gather(bf16[1,4,6]{2,1,0:T(4,128)(2,1)S(1)} %bitcast.31), channel_id=1, replica_groups=mesh['grp'=16,'shard'=32] {'shard'}, dimensions={0}, use_global_device_ids=true | all-gather | bytes 1584 | tf_op jit(solution)/shard_map/all_gather | solution.py:22
  117.5 0.1 copy.19
  118.2 0.0 copy-done.1
  118.3 0.6 gather_fusion.1
  118.9 0.1 select_convert_fusion
  118.9 61.3 %all-gather.7.cloned.1.call-done = bf16[6,128,5376]{2,0,1:T(8,128)(2,1)} async-done(((bf16[6,4,5376]{2,0,1:T(8,128)(2,1)}), bf16[6,128,5376]{2,0,1:T(8,128)(2,1)}) %all-gather.7.cloned.1.call-update) | async-done | bytes 8257552 | tf_op jit(solution)/shard_map/all_gather | solution.py:21
  180.2 8.4 %fusion = f32[6,128,3,128]{3,1,2,0:T(8,128)S(1)} fusion(bf16[6,128,5376,1]{2,0,1,3:T(8,128)(2,1)} %bitcast.35, bf16[1,1,3,5376,128]{4,3,2,1,0:T(8,128)(2,1)} %param.8), kind=kOutput, calls=%fused_computation.4 | convolution fusion | flops 3170893824 | bytes 13565952 | tf_op jit(solution)/shard_map/rd,edc->rec/dot_general | solution.py:36
  188.6 0.7 gather_fusion.3
  189.3 1.2 fusion.4
  (5 shorter events, 0.0 us)
Async XLA Ops:
  6.5 60.4 %copy-start = (bf16[8,4]{0,1:T(4,128)(2,1)S(1)}, bf16[8,4]{0,1:T(4,128)(2,1)}, u32[]{:S(2)}) copy-start(bf16[8,4]{0,1:T(4,128)(2,1)} %param.7) | copy-start | bytes 196
  6.5 56.1 %all-gather.5.cloned.1.call-start = ((), (), s32[]{:S(2)}) async-start(), calls=%async_computation | async-start | bytes 5849088 | tf_op jit(solution)/shard_map/all_gather | solution.py:13
  7.3 111.0 %copy-start.1 = (s32[1,1,18,2]{2,3,1,0:T(2,128)S(1)}, s32[1,1,18,2]{2,3,1,0:T(2,128)}, u32[]{:S(2)}) copy-start(s32[1,1,18,2]{2,3,1,0:T(2,128)} %param.10) | copy-start | bytes 436
  7.3 172.9 %all-gather.7.cloned.1.call-start = ((), (), s32[]{:S(2)}) async-start(), calls=%async_computation.1 | async-start | bytes 11354112 | tf_op jit(solution)/shard_map/all_gather | solution.py:21
Sparse Core Ops, SparseCore 0:
  9.5 53.1 all-gather.4
  67.1 113.0 all-gather.6
where the time goes:
time: 198 us; the launch traced here: 197 us
  waiting for transfers between devices  115 us (58%)
  blocking collectives  49.6 us (25%)
  between operations  14.2 us (7%)
  matrix products  8.42 us (4%)
  local copies, waits for them, and re-layouts  6.26 us (3%)
  other arithmetic  3.4 us (2%)
    all_gather x1, waiting for transfers between devices, local(): lax.all_gather(slot_rows, 'shard', axis=1, tiled=True)  61.3 us
    all_gather x1, waiting for transfers between devices, local(): lax.all_gather(src_rows, 'grp', axis=0, tiled=True)  53.5 us
    all_gather x1, blocking collectives, local(): lax.all_gather(slot_scale, 'shard', axis=1, tiled=True)  33.3 us
    all_gather x1, blocking collectives, local(): lax.all_gather(src_act, 'grp', axis=0, tiled=True)  16.3 us
    dot_general x1, matrix products, local(): jnp.einsum('rd,edc->rec', stacked, weights, preferred_element_type=jnp.fl...  8.42 us
  transfers between devices with their start and end apart: 2, of which 2 were waited for; matrix products, arithmetic and copies ran while one was open for 2% of the time, Pallas kernels for 0%

commit v1 on v0

--- a/solution.py
+++ b/solution.py
@@ -2,6 +2,27 @@
 import jax.numpy as jnp
 from jax import lax
 from jax.sharding import PartitionSpec as P
+
+
+def ring_gather(x, axis, dim):
+    devices, index, rows = (lax.axis_size(axis), lax.axis_index(axis), x.shape[dim])
+    forward = [(i, (i + 1) % devices) for i in range(devices)]
+    left = [(i, (i - 1) % devices) for i in range(devices)]
+    out = jnp.zeros((*x.shape[:dim], devices * rows, *x.shape[dim + 1 :]), x.dtype)
+    out = lax.dynamic_update_slice_in_dim(out, x, index * rows, axis=dim)
+    from_left = from_right = x
+    middle = devices // 2
+    for lap in range(1, middle + 1):
+        from_left = lax.ppermute(from_left, axis, forward)
+        out = lax.dynamic_update_slice_in_dim(
+            out, from_left, (index - lap) % devices * rows, axis=dim
+        )
+        if lap < devices - middle:
+            from_right = lax.ppermute(from_right, axis, left)
+            out = lax.dynamic_update_slice_in_dim(
+                out, from_right, (index + lap) % devices * rows, axis=dim
+            )
+    return out
 
 
 def local(src_rows, src_act, encoder, dest_list, pair_list, pair_count):
@@ -10,7 +31,7 @@
     is_valid = my_list >= 0
     picked = jnp.maximum(my_list, 0)
     all_rows, all_scale = (
-        lax.all_gather(src_rows, "grp", axis=0, tiled=True),
+        ring_gather(src_rows, "grp", 0),
         lax.all_gather(src_act, "grp", axis=0, tiled=True),
     )
     slot_rows = jnp.take(all_rows, picked, axis=0)

time: 198 us -> 213 us (1.076)
  waiting for transfers between devices: 115 us -> 69 us
  starting transfers between devices: 0.04 us -> 40.9 us
  local copies, waits for them, and re-layouts: 6.26 us -> 23.8 us
  blocking collectives: 49.6 us -> 55 us
    all_gather x1 -> x0, waiting for transfers between devices: 53.5 us -> none  [local(): lax.all_gather(src_rows, 'grp', axis=0, tiled=True)]
    ppermute x0 -> x15, starting transfers between devices: none -> 40.9 us  [the longest x7 35.2 us: ring_gather(): from_right = lax.ppermute(from_right, axis, left)]
    dynamic_update_slice x0 -> x16, local copies, waits for them, and re-layouts: none -> 13.7 us  [the longest x8 6.81 us: ring_gather(): lax.dynamic_update_slice_in_dim(out, from_left, (index - lap) % devices *...]
    ppermute x0 -> x15, waiting for transfers between devices: none -> 5.69 us  [the longest x8 5.62 us: ring_gather(): from_left = lax.ppermute(from_left, axis, forward)]
    all_gather x1, blocking collectives: 16.3 us -> 20.8 us  [local(): lax.all_gather(src_act, 'grp', axis=0, tiled=True)]
    broadcast_in_dim x0 -> x1, local copies, waits for them, and re-layouts: none -> 3.82 us  [ring_gather(): jnp.zeros((*x.shape[:dim], devices * rows, *x.shape[dim + 1:]), x.dtype)]
  transfers between devices with their start and end apart: 2 -> 16, of which waited for: 2 -> 2; matrix products, arithmetic and copies ran while one was open for 2% -> 9% of each run, Pallas kernels for 0% -> 0%
where the time goes in v1:
time: 213 us
  waiting for transfers between devices  69 us (32%)
  blocking collectives  55 us (26%)
  starting transfers between devices  40.9 us (19%)
  local copies, waits for them, and re-layouts  23.8 us (11%)
  between operations  14.2 us (7%)
  matrix products  8.42 us (4%)
    all_gather x1, waiting for transfers between devices, local(): lax.all_gather(slot_rows, 'shard', axis=1, tiled=True)  63.3 us
    ppermute x7, starting transfers between devices, ring_gather(): from_right = lax.ppermute(from_right, axis, left)  35.2 us
    all_gather x1, blocking collectives, local(): lax.all_gather(slot_scale, 'shard', axis=1, tiled=True)  34.2 us
    all_gather x1, blocking collectives, local(): lax.all_gather(src_act, 'grp', axis=0, tiled=True)  20.8 us
    dot_general x1, matrix products, local(): jnp.einsum('rd,edc->rec', stacked, weights, preferred_element_type=jnp.fl...  8.42 us
    dynamic_update_slice x8, local copies, waits for them, and re-layouts, ring_gather(): lax.dynamic_update_slice_in_dim(out, from_left, (index - lap) % devices *...  6.81 us
    dynamic_update_slice x7, local copies, waits for them, and re-layouts, ring_gather(): lax.dynamic_update_slice_in_dim(out, from_right, (index + lap) % devices...  6.02 us
    ppermute x8, starting transfers between devices, ring_gather(): from_left = lax.ppermute(from_left, axis, forward)  5.67 us
  transfers between devices with their start and end apart: 16, of which 2 were waited for; matrix products, arithmetic and copies ran while one was open for 9% of the time, Pallas kernels for 0%

profile of v1, /device:TPU:1, one launch (start us, length us, event | category | flops | bytes accessed | tf_op | source)
XLA Modules:
  0.0 213.3 jit_solution(12422634025235737951)
XLA Ops:
  6.5 3.5 %collective-permute-start = (bf16[8,4,5376]{2,1,0:T(4,128)(2,1)}, bf16[8,4,5376]{2,1,0:T(4,128)(2,1)S(1)}, u32[]{:S(2)}, u32[]{:S(2)}) collective-permute-start(bf16[8,4,5376]{2,1,0:T(4,128)(2,1)} %param.6), channel_id=1, source_target_pairs={{0,32},{32,64},{64,96},{96,128},{128,160},{160,192},{192,224},{224... | collective-permute-start | bytes 1032200 | tf_op jit(solution)/shard_map/ppermute | solution.py:16
  10.0 3.4 %collective-permute-start.1 = (bf16[8,4,5376]{2,1,0:T(4,128)(2,1)}, bf16[8,4,5376]{2,1,0:T(4,128)(2,1)S(1)}, u32[]{:S(2)}, u32[]{:S(2)}) collective-permute-start(bf16[8,4,5376]{2,1,0:T(4,128)(2,1)} %param.6), channel_id=1, source_target_pairs={{0,480},{32,0},{64,32},{96,64},{128,96},{160,128},{192,160},{224,1... | collective-permute-start | bytes 1032200 | tf_op jit(solution)/shard_map/ppermute | solution.py:21
  13.4 3.8 %broadcast_in_dim.80 = bf16[128,4,5376]{2,1,0:T(4,128)(2,1)} broadcast(bf16[]{:T(256)} %constant.145.clone.1), dimensions={} | broadcast | bytes 5505026 | tf_op jit(solution)/shard_map/broadcast_in_dim | solution.py:11
  17.2 0.8 constant_dynamic-update-slice_fusion.15
  18.5 3.2 %collective-permute-start.3 = (bf16[8,4,5376]{2,1,0:T(4,128)(2,1)S(1)}, bf16[8,4,5376]{2,1,0:T(4,128)(2,1)S(1)}, u32[]{:S(2)}, u32[]{:S(2)}) collective-permute-start(bf16[8,4,5376]{2,1,0:T(4,128)(2,1)S(1)} %collective-permute-done.1), channel_id=1, source_target_pairs={{0,480},{32,0},{64,32},{96,64},{128,96},{160,128},{192,160},{224,1... | collective-permute-start | bytes 1032200 | tf_op jit(solution)/shard_map/ppermute | solution.py:21
  21.7 0.8 constant_dynamic-update-slice_fusion.14
  22.6 0.9 constant_dynamic-update-slice_fusion.13
  23.4 1.7 collective-permute-start.4
  25.2 4.4 %collective-permute-start.5 = (bf16[8,4,5376]{2,1,0:T(4,128)(2,1)S(1)}, bf16[8,4,5376]{2,1,0:T(4,128)(2,1)S(1)}, u32[]{:S(2)}, u32[]{:S(2)}) collective-permute-start(bf16[8,4,5376]{2,1,0:T(4,128)(2,1)S(1)} %collective-permute-done.3), channel_id=1, source_target_pairs={{0,480},{32,0},{64,32},{96,64},{128,96},{160,128},{192,160},{224,1... | collective-permute-start | bytes 1032200 | tf_op jit(solution)/shard_map/ppermute | solution.py:21
  29.6 0.9 constant_dynamic-update-slice_fusion.12
  30.5 0.9 constant_dynamic-update-slice_fusion.11
  31.9 5.6 %collective-permute-start.7 = (bf16[8,4,5376]{2,1,0:T(4,128)(2,1)S(1)}, bf16[8,4,5376]{2,1,0:T(4,128)(2,1)S(1)}, u32[]{:S(2)}, u32[]{:S(2)}) collective-permute-start(bf16[8,4,5376]{2,1,0:T(4,128)(2,1)S(1)} %collective-permute-done.5), channel_id=1, source_target_pairs={{0,480},{32,0},{64,32},{96,64},{128,96},{160,128},{192,160},{224,1... | collective-permute-start | bytes 1032200 | tf_op jit(solution)/shard_map/ppermute | solution.py:21
  37.5 0.8 constant_dynamic-update-slice_fusion.10
  39.2 6.2 %collective-permute-start.9 = (bf16[8,4,5376]{2,1,0:T(4,128)(2,1)S(1)}, bf16[8,4,5376]{2,1,0:T(4,128)(2,1)S(1)}, u32[]{:S(2)}, u32[]{:S(2)}) collective-permute-start(bf16[8,4,5376]{2,1,0:T(4,128)(2,1)S(1)} %collective-permute-done.7), channel_id=1, source_target_pairs={{0,480},{32,0},{64,32},{96,64},{128,96},{160,128},{192,160},{224,1... | collective-permute-start | bytes 1032200 | tf_op jit(solution)/shard_map/ppermute | solution.py:21
  45.4 0.9 constant_dynamic-update-slice_fusion.8
  46.3 0.9 constant_dynamic-update-slice_fusion.7
  47.1 6.1 %collective-permute-start.11 = (bf16[8,4,5376]{2,1,0:T(4,128)(2,1)S(1)}, bf16[8,4,5376]{2,1,0:T(4,128)(2,1)S(1)}, u32[]{:S(2)}, u32[]{:S(2)}) collective-permute-start(bf16[8,4,5376]{2,1,0:T(4,128)(2,1)S(1)} %collective-permute-done.9), channel_id=1, source_target_pairs={{0,480},{32,0},{64,32},{96,64},{128,96},{160,128},{192,160},{224,1... | collective-permute-start | bytes 1032200 | tf_op jit(solution)/shard_map/ppermute | solution.py:21
  53.3 0.8 constant_dynamic-update-slice_fusion.6
  54.1 0.8 constant_dynamic-update-slice_fusion.5
  55.0 6.2 %collective-permute-start.13 = (bf16[8,4,5376]{2,1,0:T(4,128)(2,1)S(1)}, bf16[8,4,5376]{2,1,0:T(4,128)(2,1)S(1)}, u32[]{:S(2)}, u32[]{:S(2)}) collective-permute-start(bf16[8,4,5376]{2,1,0:T(4,128)(2,1)S(1)} %collective-permute-done.11), channel_id=1, source_target_pairs={{0,480},{32,0},{64,32},{96,64},{128,96},{160,128},{192,160},{224,1... | collective-permute-start | bytes 1032200 | tf_op jit(solution)/shard_map/ppermute | solution.py:21
  61.2 0.8 constant_dynamic-update-slice_fusion.4
  62.0 0.8 constant_dynamic-update-slice_fusion.3
  62.9 0.8 constant_dynamic-update-slice_fusion.2
  63.7 0.9 constant_dynamic-update-slice_fusion.1
  64.6 5.6 %collective-permute-done.14 = bf16[8,4,5376]{2,1,0:T(4,128)(2,1)S(1)} collective-permute-done((bf16[8,4,5376]{2,1,0:T(4,128)(2,1)S(1)}, bf16[8,4,5376]{2,1,0:T(4,128)(2,1)S(1)}, u32[]{:S(2)}, u32[]{:S(2)}) %collective-permute-start.14) | collective-permute-done | bytes 344096 | tf_op jit(solution)/shard_map/ppermute | solution.py:16
  70.2 0.8 constant_dynamic-update-slice_fusion
  71.0 3.3 %gather_fusion.2 = bf16[6,4,5376]{2,1,0:T(4,128)(2,1)S(1)} fusion(bf16[128,4,5376]{2,1,0:T(4,128)(2,1)} %constant_dynamic-update-slice_fusion, s32[1024]{0:T(1024)S(1)} %pad_clamp_fusion.1), kind=kCustom, calls=%fused_computation.2 | custom fusion | bytes 516120 | tf_op jit(solution)/shard_map/jit(_take)/gather | solution.py:37
  75.4 20.8 %all-gather = bf16[16,8,4]{1,2,0:T(4,128)(2,1)S(1)} all-gather(bf16[1,8,4]{1,2,0:T(4,128)(2,1)S(1)} %bitcast.32), channel_id=1, replica_groups=mesh['grp'=16,'shard'=32] {'grp'}, dimensions={0}, use_global_device_ids=true | all-gather | bytes 1088 | tf_op jit(solution)/shard_map/all_gather | solution.py:35
  97.1 34.2 %all-gather.1 = bf16[32,4,6]{2,1,0:T(4,128)(2,1)S(1)} all-gather(bf16[1,4,6]{2,1,0:T(4,128)(2,1)S(1)} %bitcast.31), channel_id=1, replica_groups=mesh['grp'=16,'shard'=32] {'shard'}, dimensions={0}, use_global_device_ids=true | all-gather | bytes 1584 | tf_op jit(solution)/shard_map/all_gather | solution.py:43
  132.8 63.3 %all-gather.4.cloned.1.call-done = bf16[6,128,5376]{2,0,1:T(8,128)(2,1)} async-done(((bf16[6,4,5376]{2,0,1:T(8,128)(2,1)}), bf16[6,128,5376]{2,0,1:T(8,128)(2,1)}) %all-gather.4.cloned.1.call-update) | async-done | bytes 8257552 | tf_op jit(solution)/shard_map/all_gather | solution.py:42
  196.1 8.4 %fusion = f32[6,128,3,128]{3,1,2,0:T(8,128)S(1)} fusion(bf16[6,128,5376,1]{2,0,1,3:T(8,128)(2,1)} %bitcast.35, bf16[1,1,3,5376,128]{4,3,2,1,0:T(8,128)(2,1)} %param.8), kind=kOutput, calls=%fused_computation.4 | convolution fusion | flops 3170893824 | bytes 13565952 | tf_op jit(solution)/shard_map/rd,edc->rec/dot_general | solution.py:57
  205.2 1.2 fusion.4
  (48 shorter events, 5.2 us)
Async XLA Ops:
  6.5 10.7 %copy-start = (bf16[8,4,5376]{2,1,0:T(4,128)(2,1)S(1)}, bf16[8,4,5376]{2,1,0:T(4,128)(2,1)}, u32[]{:S(2)}) copy-start(bf16[8,4,5376]{2,1,0:T(4,128)(2,1)} %param.6) | copy-start | bytes 1032196
  6.5 11.5 %copy-start.1 = (s32[16,6]{0,1:T(8,128)S(1)}, s32[16,6]{0,1:T(8,128)}, u32[]{:S(2)}) copy-start(s32[16,6]{0,1:T(8,128)} %param.9) | copy-start | bytes 1156
  6.5 189.6 %all-gather.4.cloned.1.call-start = ((), (), s32[]{:S(2)}) async-start(), calls=%async_computation | async-start | bytes 11354112 | tf_op jit(solution)/shard_map/all_gather | solution.py:42
  6.5 11.9 %collective-permute-start = (bf16[8,4,5376]{2,1,0:T(4,128)(2,1)}, bf16[8,4,5376]{2,1,0:T(4,128)(2,1)S(1)}, u32[]{:S(2)}, u32[]{:S(2)}) collective-permute-start(bf16[8,4,5376]{2,1,0:T(4,128)(2,1)} %param.6), channel_id=1, source_target_pairs={{0,32},{32,64},{64,96},{96,128},{128,160},{160,192},{192,224},{224... | collective-permute-start | bytes 1032200 | tf_op jit(solution)/shard_map/ppermute | solution.py:16
  10.0 8.5 %collective-permute-start.1 = (bf16[8,4,5376]{2,1,0:T(4,128)(2,1)}, bf16[8,4,5376]{2,1,0:T(4,128)(2,1)S(1)}, u32[]{:S(2)}, u32[]{:S(2)}) collective-permute-start(bf16[8,4,5376]{2,1,0:T(4,128)(2,1)} %param.6), channel_id=1, source_target_pairs={{0,480},{32,0},{64,32},{96,64},{128,96},{160,128},{192,160},{224,1... | collective-permute-start | bytes 1032200 | tf_op jit(solution)/shard_map/ppermute | solution.py:21
  18.5 5.0 %collective-permute-start.2 = (bf16[8,4,5376]{2,1,0:T(4,128)(2,1)S(1)}, bf16[8,4,5376]{2,1,0:T(4,128)(2,1)S(1)}, u32[]{:S(2)}, u32[]{:S(2)}) collective-permute-start(bf16[8,4,5376]{2,1,0:T(4,128)(2,1)S(1)} %collective-permute-done), channel_id=1, source_target_pairs={{0,32},{32,64},{64,96},{96,128},{128,160},{160,192},{192,224},{224... | collective-permute-start | bytes 1032200 | tf_op jit(solution)/shard_map/ppermute | solution.py:16
  18.5 6.7 %collective-permute-start.3 = (bf16[8,4,5376]{2,1,0:T(4,128)(2,1)S(1)}, bf16[8,4,5376]{2,1,0:T(4,128)(2,1)S(1)}, u32[]{:S(2)}, u32[]{:S(2)}) collective-permute-start(bf16[8,4,5376]{2,1,0:T(4,128)(2,1)S(1)} %collective-permute-done.1), channel_id=1, source_target_pairs={{0,480},{32,0},{64,32},{96,64},{128,96},{160,128},{192,160},{224,1... | collective-permute-start | bytes 1032200 | tf_op jit(solution)/shard_map/ppermute | solution.py:21
  23.4 51.9 %copy-start.2 = (bf16[8,4]{0,1:T(4,128)(2,1)S(1)}, bf16[8,4]{0,1:T(4,128)(2,1)}, u32[]{:S(2)}) copy-start(bf16[8,4]{0,1:T(4,128)(2,1)} %param.7) | copy-start | bytes 196
  23.4 108.6 %copy-start.3 = (s32[1,1,18,2]{2,3,1,0:T(2,128)S(1)}, s32[1,1,18,2]{2,3,1,0:T(2,128)}, u32[]{:S(2)}) copy-start(s32[1,1,18,2]{2,3,1,0:T(2,128)} %param.10) | copy-start | bytes 436
  23.4 7.9 %collective-permute-start.4 = (bf16[8,4,5376]{2,1,0:T(4,128)(2,1)S(1)}, bf16[8,4,5376]{2,1,0:T(4,128)(2,1)S(1)}, u32[]{:S(2)}, u32[]{:S(2)}) collective-permute-start(bf16[8,4,5376]{2,1,0:T(4,128)(2,1)S(1)} %collective-permute-done.2), channel_id=1, source_target_pairs={{0,32},{32,64},{64,96},{96,128},{128,160},{160,192},{192,224},{224... | collective-permute-start | bytes 1032200 | tf_op jit(solution)/shard_map/ppermute | solution.py:16
  25.2 6.7 %collective-permute-start.5 = (bf16[8,4,5376]{2,1,0:T(4,128)(2,1)S(1)}, bf16[8,4,5376]{2,1,0:T(4,128)(2,1)S(1)}, u32[]{:S(2)}, u32[]{:S(2)}) collective-permute-start(bf16[8,4,5376]{2,1,0:T(4,128)(2,1)S(1)} %collective-permute-done.3), channel_id=1, source_target_pairs={{0,480},{32,0},{64,32},{96,64},{128,96},{160,128},{192,160},{224,1... | collective-permute-start | bytes 1032200 | tf_op jit(solution)/shard_map/ppermute | solution.py:21
  31.4 7.8 %collective-permute-start.6 = (bf16[8,4,5376]{2,1,0:T(4,128)(2,1)S(1)}, bf16[8,4,5376]{2,1,0:T(4,128)(2,1)S(1)}, u32[]{:S(2)}, u32[]{:S(2)}) collective-permute-start(bf16[8,4,5376]{2,1,0:T(4,128)(2,1)S(1)} %collective-permute-done.4), channel_id=1, source_target_pairs={{0,32},{32,64},{64,96},{96,128},{128,160},{160,192},{192,224},{224... | collective-permute-start | bytes 1032200 | tf_op jit(solution)/shard_map/ppermute | solution.py:16
  31.9 7.3 %collective-permute-start.7 = (bf16[8,4,5376]{2,1,0:T(4,128)(2,1)S(1)}, bf16[8,4,5376]{2,1,0:T(4,128)(2,1)S(1)}, u32[]{:S(2)}, u32[]{:S(2)}) collective-permute-start(bf16[8,4,5376]{2,1,0:T(4,128)(2,1)S(1)} %collective-permute-done.5), channel_id=1, source_target_pairs={{0,480},{32,0},{64,32},{96,64},{128,96},{160,128},{192,160},{224,1... | collective-permute-start | bytes 1032200 | tf_op jit(solution)/shard_map/ppermute | solution.py:21
  39.2 7.9 %collective-permute-start.8 = (bf16[8,4,5376]{2,1,0:T(4,128)(2,1)S(1)}, bf16[8,4,5376]{2,1,0:T(4,128)(2,1)S(1)}, u32[]{:S(2)}, u32[]{:S(2)}) collective-permute-start(bf16[8,4,5376]{2,1,0:T(4,128)(2,1)S(1)} %collective-permute-done.6), channel_id=1, source_target_pairs={{0,32},{32,64},{64,96},{96,128},{128,160},{160,192},{192,224},{224... | collective-permute-start | bytes 1032200 | tf_op jit(solution)/shard_map/ppermute | solution.py:16
  39.2 7.9 %collective-permute-start.9 = (bf16[8,4,5376]{2,1,0:T(4,128)(2,1)S(1)}, bf16[8,4,5376]{2,1,0:T(4,128)(2,1)S(1)}, u32[]{:S(2)}, u32[]{:S(2)}) collective-permute-start(bf16[8,4,5376]{2,1,0:T(4,128)(2,1)S(1)} %collective-permute-done.7), channel_id=1, source_target_pairs={{0,480},{32,0},{64,32},{96,64},{128,96},{160,128},{192,160},{224,1... | collective-permute-start | bytes 1032200 | tf_op jit(solution)/shard_map/ppermute | solution.py:21
  47.1 7.9 %collective-permute-start.10 = (bf16[8,4,5376]{2,1,0:T(4,128)(2,1)S(1)}, bf16[8,4,5376]{2,1,0:T(4,128)(2,1)S(1)}, u32[]{:S(2)}, u32[]{:S(2)}) collective-permute-start(bf16[8,4,5376]{2,1,0:T(4,128)(2,1)S(1)} %collective-permute-done.8), channel_id=1, source_target_pairs={{0,32},{32,64},{64,96},{96,128},{128,160},{160,192},{192,224},{224... | collective-permute-start | bytes 1032200 | tf_op jit(solution)/shard_map/ppermute | solution.py:16
  47.1 7.9 %collective-permute-start.11 = (bf16[8,4,5376]{2,1,0:T(4,128)(2,1)S(1)}, bf16[8,4,5376]{2,1,0:T(4,128)(2,1)S(1)}, u32[]{:S(2)}, u32[]{:S(2)}) collective-permute-start(bf16[8,4,5376]{2,1,0:T(4,128)(2,1)S(1)} %collective-permute-done.9), channel_id=1, source_target_pairs={{0,480},{32,0},{64,32},{96,64},{128,96},{160,128},{192,160},{224,1... | collective-permute-start | bytes 1032200 | tf_op jit(solution)/shard_map/ppermute | solution.py:21
  55.0 7.9 %collective-permute-start.12 = (bf16[8,4,5376]{2,1,0:T(4,128)(2,1)S(1)}, bf16[8,4,5376]{2,1,0:T(4,128)(2,1)S(1)}, u32[]{:S(2)}, u32[]{:S(2)}) collective-permute-start(bf16[8,4,5376]{2,1,0:T(4,128)(2,1)S(1)} %collective-permute-done.10), channel_id=1, source_target_pairs={{0,32},{32,64},{64,96},{96,128},{128,160},{160,192},{192,224},{224... | collective-permute-start | bytes 1032200 | tf_op jit(solution)/shard_map/ppermute | solution.py:16
  55.0 8.7 %collective-permute-start.13 = (bf16[8,4,5376]{2,1,0:T(4,128)(2,1)S(1)}, bf16[8,4,5376]{2,1,0:T(4,128)(2,1)S(1)}, u32[]{:S(2)}, u32[]{:S(2)}) collective-permute-start(bf16[8,4,5376]{2,1,0:T(4,128)(2,1)S(1)} %collective-permute-done.11), channel_id=1, source_target_pairs={{0,480},{32,0},{64,32},{96,64},{128,96},{160,128},{192,160},{224,1... | collective-permute-start | bytes 1032200 | tf_op jit(solution)/shard_map/ppermute | solution.py:21
  62.9 7.3 %collective-permute-start.14 = (bf16[8,4,5376]{2,1,0:T(4,128)(2,1)S(1)}, bf16[8,4,5376]{2,1,0:T(4,128)(2,1)S(1)}, u32[]{:S(2)}, u32[]{:S(2)}) collective-permute-start(bf16[8,4,5376]{2,1,0:T(4,128)(2,1)S(1)} %collective-permute-done.12), channel_id=1, source_target_pairs={{0,32},{32,64},{64,96},{96,128},{128,160},{160,192},{192,224},{224... | collective-permute-start | bytes 1032200 | tf_op jit(solution)/shard_map/ppermute | solution.py:16
Sparse Core Ops, SparseCore 0:
  75.5 120.5 all-gather.3
